TPU v7x, 256 devices: a whole 4x4x8 slice. The times are simulated.
256 devices in a mesh: gx: 16 (over z, core), gy: 16 (over x, y).
Axes of the slice: x: 4, y: 4, z: 8, core: 2. Of those that a mesh axis runs over, the one named last changes fastest.
Arguments:
- forcing: float32 [4, 8, 4096, 2048], P(None, None, 'gx', 'gy'), may hold values from -150 to 150
- velocity: float32 [2, 4096, 2048], P(None, 'gx', 'gy'), may hold values from -0.6 to 0.6
- viscosity: float32 [4096, 2048], P('gx', 'gy'), may hold values from 0.05 to 0.25
- sound: float32 [4096, 2048], P('gx', 'gy'), may hold values from 0.4 to 1
- coupling: float32 [4, 4, 4096, 2048], P(None, None, 'gx', 'gy'), may hold values from -1.5 to 1.5
Outputs:
- basis: float32 [4, 8, 4096, 2048], P(None, None, 'gx', 'gy')
- factor: float32 [8, 8], replicated
All inputs are finite; a program needn't handle non-finite values.
Results may differ from a plain program's by a relative error of at most 0.000055.
Values sent between devices are 32-bit elements; how exact they have to be, the bound alone decides.
No kernel may reach another device: no remote copies, remote signals or barrier semaphores. Data moves between devices by JAX's collectives and lax.ppermute only.
A program may use at most 128 MiB of HBM per device.

v0:
```python
import jax
import jax.numpy as jnp
from jax import lax
from jax.sharding import PartitionSpec as P

STEP = 0.5


def with_halo(cells, sides, width):
    for axis, dim in sides:
        count = lax.axis_size(axis)
        ends = count - 1
        head = lax.slice_in_dim(cells, 0, width, axis=dim)
        tail = lax.slice_in_dim(cells, cells.shape[dim] - width, cells.shape[dim], axis=dim)
        cells = jnp.concatenate(
            [
                lax.ppermute(tail, axis, [(i, (i + 1) % count) for i in range(ends)]),
                cells,
                lax.ppermute(head, axis, [((i + 1) % count, i) for i in range(ends)]),
            ],
            axis=dim,
        )
    return cells


def tendency(padded, velocity, viscosity, sound, coupling):
    center = padded[:, :, 1:-1, 1:-1]
    east = padded[:, :, 2:, 1:-1]
    west = padded[:, :, :-2, 1:-1]
    north = padded[:, :, 1:-1, 2:]
    south = padded[:, :, 1:-1, :-2]
    grad_x = 0.5 * (east - west)
    grad_y = 0.5 * (north - south)
    laplace = east + west + north + south - 4.0 * center
    transport = viscosity * laplace - velocity[0] * grad_x - velocity[1] * grad_y
    divergence = grad_x[1] + grad_y[2]
    acoustic = jnp.stack(
        [-sound * divergence, -sound * grad_x[3], -sound * grad_y[3], -sound * divergence]
    )
    mixing = coupling[:, 0][:, None] * center[0][None]
    for inner in range(1, 4):
        mixing = mixing + coupling[:, inner][:, None] * center[inner][None]
    return transport + acoustic - mixing


def extend(state):
    return with_halo(state, (("gx", 2), ("gy", 3)), 1)


def local(forcing, velocity, viscosity, sound, coupling):
    first = tendency(extend(forcing), velocity, viscosity, sound, coupling) + forcing
    middle = forcing + STEP * first
    second = tendency(extend(middle), velocity, viscosity, sound, coupling) + forcing
    response = forcing + 0.5 * STEP * (first + second)
    rows_total = float(
        4 * forcing.shape[2] * forcing.shape[3] * lax.axis_size("gx") * lax.axis_size("gy")
    )
    local_gram = (
        jnp.einsum("vcxy,vdxy->cd", response, response, precision=lax.Precision.HIGHEST)
        / rows_total
    )
    lower = jnp.linalg.cholesky(lax.psum(local_gram, ("gx", "gy")))
    identity = jnp.eye(lower.shape[0], dtype=lower.dtype)
    inverse = lax.linalg.triangular_solve(lower, identity, left_side=True, lower=True)
    basis = jnp.einsum("cd,vdxy->vcxy", inverse, response, precision=lax.Precision.HIGHEST)
    return (basis, lower.T)


def solution(mesh):
    in_specs = (
        P(None, None, "gx", "gy"),
        P(None, "gx", "gy"),
        P("gx", "gy"),
        P("gx", "gy"),
        P(None, None, "gx", "gy"),
    )
    out_specs = (P(None, None, "gx", "gy"), P())
    return jax.shard_map(local, mesh=mesh, in_specs=in_specs, out_specs=out_specs, check_vma=False)
```

profile of v0, /device:TPU:1, one launch (start us, length us, event | category | flops | bytes accessed | tf_op | source)
XLA Modules:
  0.0 236.0 jit_solution(18305960756760041180)
XLA Ops:
  1.6 5.1 %collective-permute-start = (f32[4,8,1,128]{3,1,2,0:T(8,128)S(1)}, f32[4,8,1,128]{3,1,2,0:T(8,128)S(1)}, u32[]{:S(2)}, u32[]{:S(2)}) collective-permute-start(f32[4,8,1,128]{3,1,2,0:T(8,128)S(1)} %bitcast.57), channel_id=1, source_target_pairs={{16,0},{32,16},{48,32},{64,48},{80,64},{96,80},{112,96},{128,112},... | collective-permute-start | bytes 49160 | tf_op jit(solution)/shard_map/ppermute | solution.py:19
  6.8 2.1 collective-permute-start.1
  8.8 3.8 %slice_bitcast_fusion.7 = (f32[8,256,128]{2,1,0:T(8,128)}, f32[8,256,128]{2,1,0:T(8,128)S(1)}, f32[8,256,128]{2,1,0:T(8,128)}, f32[8,256,128]{2,1,0:T(8,128)}) fusion(f32[4,8,256,128]{3,2,1,0:T(8,128)} %param.5), kind=kLoop, calls=%fused_computation.51 | loop fusion | bytes 8388608 | tf_op jit(solution)/shard_map/mul | solution.py:40
  14.1 5.4 %copy.76 = f32[4,8,256,128]{2,1,3,0:T(8,128)} copy(f32[4,8,256,128]{3,2,1,0:T(8,128)} %param.5) | data formatting | bytes 8388608 | tf_op args[0]
  23.8 3.6 %collective-permute-start.3 = (f32[4,8,258,1]{2,1,3,0:T(8,128)}, f32[4,8,258,1]{2,1,3,0:T(8,128)}, u32[]{:S(2)}, u32[]{:S(2)}) collective-permute-start(f32[4,8,258,1]{2,1,3,0:T(8,128)} %get-tuple-element.16), channel_id=1, source_target_pairs={{0,1},{1,2},{2,3},{3,4},{4,5},{5,6},{6,7},{7,8},{8,9},{9,10},{10,1... | collective-permute-start | bytes 99080 | tf_op jit(solution)/shard_map/ppermute | solution.py:17
  31.4 2.6 %copy.64 = f32[8,256,128]{1,0,2:T(8,128)} copy(f32[8,256,128]{2,1,0:T(8,128)} %get-tuple-element.35) | data formatting | bytes 2097152 | tf_op jit(solution)/shard_map/mul | solution.py:42
  35.3 2.6 %copy.62 = f32[8,256,128]{1,0,2:T(8,128)} copy(f32[8,256,128]{2,1,0:T(8,128)} %get-tuple-element.34) | data formatting | bytes 2097152 | tf_op jit(solution)/shard_map/mul | solution.py:42
  37.9 2.0 copy.61
  39.9 2.7 %copy.60 = f32[8,256,128]{1,0,2:T(8,128)} copy(f32[8,256,128]{2,1,0:T(8,128)} %get-tuple-element.32) | data formatting | bytes 2097152 | tf_op jit(solution)/shard_map/mul | solution.py:40
  47.6 10.8 %fusion.8 = (f32[4,8,256,128]{2,1,3,0:T(8,128)S(1)}, f32[4,8,256,128]{2,1,3,0:T(8,128)S(1)}) fusion(f32[4,8,1,128]{2,1,3,0:T(8,128)S(1)} %copy.48, f32[4,8,256,128]{2,1,3,0:T(8,128)} %copy.76, f32[4,8,1,128]{2,1,3,0:T(8,128)} %copy.50, f32[4,8,258,1]{2,1,3,0:T(8,128)} %collective-permute-done.3, f32[4,8,258,1]{2,1,3,0:T(8,128)} %collective-permute-done.2), kind=kLoop, calls=%fused_computation.27 | loop fusion | flops 12582912 | bytes 12681728 | tf_op jit(solution)/shard_map/mul | solution.py:32
  62.4 11.5 %multiply_add_fusion = (f32[4,8,256,128]{2,1,3,0:T(8,128)S(1)}, f32[4,8,256,128]{2,1,3,0:T(8,128)}) fusion(f32[4,8,256,128]{2,1,3,0:T(8,128)S(1)} %copy-done.2, f32[8,256,128]{1,0,2:T(8,128)} %copy.66, f32[4,256,128]{1,2,0:T(8,128)S(1)} %copy.65, f32[8,256,128]{1,0,2:T(8,128)} %copy.64, f32[4,256,128]{1,2,0:T(8,128)S(1)} %copy.63, f32[8,256,128]{1,0,2:T(8,128)} %copy.62, ...), kind=kLoop, calls=%fused_computation.25 | loop fusion | flops 36700160 | bytes 22512128 | tf_op jit(solution)/shard_map/add | solution.py:52
  73.9 2.5 %fusion.18 = (f32[4,8,1,128]{2,1,3,0:T(8,128)S(1)}, f32[4,8,1,128]{2,1,3,0:T(8,128)}) fusion(f32[4,8,256,128]{2,1,3,0:T(8,128)S(1)} %get-tuple-element.8), kind=kLoop, calls=%fused_computation.74 | loop fusion | bytes 65536 | tf_op jit(solution)/shard_map/slice | solution.py:14
  76.6 2.2 copy.69
  82.0 3.6 %collective-permute-start.5 = (f32[4,8,1,128]{3,1,2,0:T(8,128)}, f32[4,8,1,128]{3,1,2,0:T(8,128)}, u32[]{:S(2)}, u32[]{:S(2)}) collective-permute-start(f32[4,8,1,128]{3,1,2,0:T(8,128)} %copy.71), channel_id=1, source_target_pairs={{0,16},{16,32},{32,48},{48,64},{64,80},{80,96},{96,112},{112,128},... | collective-permute-start | bytes 49160 | tf_op jit(solution)/shard_map/ppermute | solution.py:17
  87.1 2.8 %copy.72 = f32[4,8,1,128]{2,1,3,0:T(8,128)} copy(f32[4,8,1,128]{3,1,2,0:T(8,128)} %collective-permute-done.5) | data formatting | bytes 32768 | tf_op jit(solution)/shard_map/ppermute | solution.py:17
  90.9 4.1 %collective-permute-start.7 = (f32[4,8,258,1]{2,1,3,0:T(8,128)S(1)}, f32[4,8,258,1]{2,1,3,0:T(8,128)S(1)}, u32[]{:S(2)}, u32[]{:S(2)}) collective-permute-start(f32[4,8,258,1]{2,1,3,0:T(8,128)S(1)} %get-tuple-element.12), channel_id=1, source_target_pairs={{0,1},{1,2},{2,3},{3,4},{4,5},{5,6},{6,7},{7,8},{8,9},{9,10},{10,1... | collective-permute-start | bytes 99080 | tf_op jit(solution)/shard_map/ppermute | solution.py:17
  100.7 6.9 %fusion.10 = (f32[4,8,256,128]{2,1,3,0:T(8,128)}, f32[4,8,256,128]{2,1,3,0:T(8,128)}) fusion(f32[4,8,1,128]{2,1,3,0:T(8,128)S(1)} %copy.70, f32[4,8,256,128]{2,1,3,0:T(8,128)S(1)} %copy-done.1, f32[4,8,1,128]{2,1,3,0:T(8,128)S(1)} %copy-done.5, f32[4,8,258,1]{2,1,3,0:T(8,128)S(1)} %collective-permute-done.7, f32[4,8,258,1]{2,1,3,0:T(8,128)S(1)} %collective-permute-done.6), kind=kLoop, calls=%fused_computation.29 | loop fusion | flops 12582912 | bytes 12681728 | tf_op jit(solution)/shard_map/mul | solution.py:32
  107.6 4.0 %slice_multiply_fusion.1 = (f32[1,8,256,128]{2,1,3,0:T(8,128)S(1)}, f32[1,8,256,128]{2,1,3,0:T(8,128)}, f32[1,8,256,128]{2,1,3,0:T(8,128)}) fusion(f32[4,8,256,128]{2,1,3,0:T(8,128)} %get-tuple-element.10, f32[256,128]{0,1:T(8,128)S(1)} %copy-done.11, f32[4,8,256,128]{2,1,3,0:T(8,128)} %get-tuple-element.11), kind=kLoop, calls=%fused_computation.41 | loop fusion | flops 1048576 | bytes 7471104 | tf_op jit(solution)/shard_map/mul | solution.py:38
  111.8 11.4 %fusion.6 = f32[4,8,256,128]{2,1,3,0:T(8,128)} fusion(f32[4,8,256,128]{2,1,3,0:T(8,128)S(1)} %copy-done.3, f32[4,8,256,128]{2,1,3,0:T(8,128)S(1)} %copy-done.6, f32[1,8,256,128]{2,1,3,0:T(8,128)} %get-tuple-element.19, f32[1,8,256,128]{2,1,3,0:T(8,128)} %get-tuple-element.20, f32[1,8,256,128]{2,1,3,0:T(8,128)S(1)} %get-tuple-element.18, ...), kind=kLoop, calls=%fused_computation.24 | loop fusion | flops 37748736 | bytes 26706432 | tf_op jit(solution)/shard_map/add | solution.py:54
  123.2 5.5 %copy.80 = f32[4,8,256,128]{3,1,2,0:T(8,128)} copy(f32[4,8,256,128]{2,1,3,0:T(8,128)} %fusion.6) | data formatting | bytes 8388608 | tf_op jit(solution)/shard_map/add | solution.py:54
  128.7 12.6 %fusion.11 = f32[8,8]{0,1:T(8,128)S(1)} fusion(f32[4,8,256,128]{2,1,3,0:T(8,128)} %fusion.6), kind=kOutput, calls=%fused_computation.35 | convolution fusion | flops 100663360 | bytes 4194560 | tf_op jit(solution)/shard_map/vcxy,vdxy->cd/dot_general | solution.py:59
  141.2 83.0 %psum.7 = f32[8,8]{0,1:T(8,128)S(1)} all-reduce(f32[8,8]{0,1:T(8,128)S(1)} %fusion.11), channel_id=1, replica_groups=mesh['gx'=16,'gy'=16] {'gx','gy'}, use_global_device_ids=true, to_apply=%region_0.0 | all-reduce | flops 64 | bytes 512 | tf_op jit(solution)/shard_map/psum | solution.py:62
  227.2 5.3 %convolution_bitcast_fusion = f32[4,8,256,128]{3,1,2,0:T(8,128)S(1)} fusion(f32[4,8,256,128]{3,1,2,0:T(8,128)} %copy.80, f32[8,8,1,1]{1,0,3,2:T(8,128)S(1)} %convolution_bitcast_fusion.1), kind=kOutput, calls=%fused_computation.30 | convolution fusion | flops 100663296 | bytes 8388864 | tf_op jit(solution)/shard_map/cd,vdxy->vcxy/dot_general | solution.py:65
  232.5 2.8 %copy.81 = f32[4,8,256,128]{3,2,1,0:T(8,128)} copy(f32[4,8,256,128]{3,1,2,0:T(8,128)S(1)} %convolution_bitcast_fusion) | data formatting | bytes 8388608
  (66 shorter events, 36.0 us)
Async XLA Ops:
  1.6 17.9 %collective-permute-start = (f32[4,8,1,128]{3,1,2,0:T(8,128)S(1)}, f32[4,8,1,128]{3,1,2,0:T(8,128)S(1)}, u32[]{:S(2)}, u32[]{:S(2)}) collective-permute-start(f32[4,8,1,128]{3,1,2,0:T(8,128)S(1)} %bitcast.57), channel_id=1, source_target_pairs={{16,0},{32,16},{48,32},{64,48},{80,64},{96,80},{112,96},{128,112},... | collective-permute-start | bytes 49160 | tf_op jit(solution)/shard_map/ppermute | solution.py:19
  6.7 5.9 %copy-start.9 = (f32[4,4,256,128]{3,2,1,0:T(8,128)S(1)}, f32[4,4,256,128]{3,2,1,0:T(8,128)}, u32[]{:S(2)}) copy-start(f32[4,4,256,128]{3,2,1,0:T(8,128)} %param.9) | copy-start | bytes 6291460
  6.8 13.5 %collective-permute-start.1 = (f32[4,8,1,128]{3,1,2,0:T(8,128)S(1)}, f32[4,8,1,128]{3,1,2,0:T(8,128)S(1)}, u32[]{:S(2)}, u32[]{:S(2)}) collective-permute-start(f32[4,8,1,128]{3,1,2,0:T(8,128)S(1)} %bitcast.56), channel_id=1, source_target_pairs={{0,16},{16,32},{32,48},{48,64},{64,80},{80,96},{96,112},{112,128},... | collective-permute-start | bytes 49160 | tf_op jit(solution)/shard_map/ppermute | solution.py:17
  22.2 6.5 %copy-start.12 = (f32[2,256,128]{2,1,0:T(8,128)S(1)}, f32[2,256,128]{2,1,0:T(8,128)}, u32[]{:S(2)}) copy-start(f32[2,256,128]{2,1,0:T(8,128)} %param.6) | copy-start | bytes 786436
  23.8 23.7 %collective-permute-start.3 = (f32[4,8,258,1]{2,1,3,0:T(8,128)}, f32[4,8,258,1]{2,1,3,0:T(8,128)}, u32[]{:S(2)}, u32[]{:S(2)}) collective-permute-start(f32[4,8,258,1]{2,1,3,0:T(8,128)} %get-tuple-element.16), channel_id=1, source_target_pairs={{0,1},{1,2},{2,3},{3,4},{4,5},{5,6},{6,7},{7,8},{8,9},{9,10},{10,1... | collective-permute-start | bytes 99080 | tf_op jit(solution)/shard_map/ppermute | solution.py:17
  27.4 20.1 %collective-permute-start.2 = (f32[4,8,258,1]{2,1,3,0:T(8,128)}, f32[4,8,258,1]{2,1,3,0:T(8,128)}, u32[]{:S(2)}, u32[]{:S(2)}) collective-permute-start(f32[4,8,258,1]{2,1,3,0:T(8,128)} %get-tuple-element.17), channel_id=1, source_target_pairs={{1,0},{2,1},{3,2},{4,3},{5,4},{6,5},{7,6},{8,7},{9,8},{10,9},{11,1... | collective-permute-start | bytes 99080 | tf_op jit(solution)/shard_map/ppermute | solution.py:19
  47.5 10.9 %copy-start.10 = (f32[256,128]{0,1:T(8,128)S(1)}, f32[256,128]{0,1:T(8,128)}, u32[]{:S(2)}) copy-start(f32[256,128]{0,1:T(8,128)} %copy.58) | copy-start | bytes 393220
  58.4 3.3 %copy-start.2 = (f32[4,8,256,128]{2,1,3,0:T(8,128)S(1)}, f32[4,8,256,128]{2,1,3,0:T(8,128)}, u32[]{:S(2)}) copy-start(f32[4,8,256,128]{2,1,3,0:T(8,128)} %copy.76) | copy-start | bytes 12582916
  58.4 4.0 %copy-start.4 = (f32[4,8,1,128]{2,1,3,0:T(8,128)S(1)}, f32[4,8,1,128]{2,1,3,0:T(8,128)}, u32[]{:S(2)}) copy-start(f32[4,8,1,128]{2,1,3,0:T(8,128)} %copy.50) | copy-start | bytes 49156
  73.9 2.7 %copy-start = (f32[4,8,256,128]{2,1,3,0:T(8,128)}, f32[4,8,256,128]{2,1,3,0:T(8,128)S(1)}, u32[]{:S(2)}) copy-start(f32[4,8,256,128]{2,1,3,0:T(8,128)S(1)} %get-tuple-element.8) | copy-start | bytes 12582916
  78.8 6.8 %collective-permute-start.4 = (f32[4,8,1,128]{3,1,2,0:T(8,128)S(1)}, f32[4,8,1,128]{3,1,2,0:T(8,128)}, u32[]{:S(2)}, u32[]{:S(2)}) collective-permute-start(f32[4,8,1,128]{3,1,2,0:T(8,128)S(1)} %copy.69), channel_id=1, source_target_pairs={{16,0},{32,16},{48,32},{64,48},{80,64},{96,80},{112,96},{128,112},... | collective-permute-start | bytes 49160 | tf_op jit(solution)/shard_map/ppermute | solution.py:19
  82.0 5.1 %collective-permute-start.5 = (f32[4,8,1,128]{3,1,2,0:T(8,128)}, f32[4,8,1,128]{3,1,2,0:T(8,128)}, u32[]{:S(2)}, u32[]{:S(2)}) collective-permute-start(f32[4,8,1,128]{3,1,2,0:T(8,128)} %copy.71), channel_id=1, source_target_pairs={{0,16},{16,32},{32,48},{48,64},{64,80},{80,96},{96,112},{112,128},... | collective-permute-start | bytes 49160 | tf_op jit(solution)/shard_map/ppermute | solution.py:17
  89.8 6.8 %copy-start.1 = (f32[4,8,256,128]{2,1,3,0:T(8,128)S(1)}, f32[4,8,256,128]{2,1,3,0:T(8,128)}, u32[]{:S(2)}) copy-start(f32[4,8,256,128]{2,1,3,0:T(8,128)} %copy-done) | copy-start | bytes 12582916
  90.9 7.8 %collective-permute-start.7 = (f32[4,8,258,1]{2,1,3,0:T(8,128)S(1)}, f32[4,8,258,1]{2,1,3,0:T(8,128)S(1)}, u32[]{:S(2)}, u32[]{:S(2)}) collective-permute-start(f32[4,8,258,1]{2,1,3,0:T(8,128)S(1)} %get-tuple-element.12), channel_id=1, source_target_pairs={{0,1},{1,2},{2,3},{3,4},{4,5},{5,6},{6,7},{7,8},{8,9},{9,10},{10,1... | collective-permute-start | bytes 99080 | tf_op jit(solution)/shard_map/ppermute | solution.py:17
  95.0 5.7 %copy-start.5 = (f32[4,8,1,128]{2,1,3,0:T(8,128)S(1)}, f32[4,8,1,128]{2,1,3,0:T(8,128)}, u32[]{:S(2)}) copy-start(f32[4,8,1,128]{2,1,3,0:T(8,128)} %copy.72) | copy-start | bytes 49156
  95.0 5.7 %collective-permute-start.6 = (f32[4,8,258,1]{2,1,3,0:T(8,128)S(1)}, f32[4,8,258,1]{2,1,3,0:T(8,128)S(1)}, u32[]{:S(2)}, u32[]{:S(2)}) collective-permute-start(f32[4,8,258,1]{2,1,3,0:T(8,128)S(1)} %get-tuple-element.13), channel_id=1, source_target_pairs={{1,0},{2,1},{3,2},{4,3},{5,4},{6,5},{7,6},{8,7},{9,8},{10,9},{11,1... | collective-permute-start | bytes 99080 | tf_op jit(solution)/shard_map/ppermute | solution.py:19
  98.6 9.0 %copy-start.11 = (f32[256,128]{0,1:T(8,128)S(1)}, f32[256,128]{0,1:T(8,128)}, u32[]{:S(2)}) copy-start(f32[256,128]{0,1:T(8,128)} %copy.58) | copy-start | bytes 393220
  100.7 10.9 %copy-start.6 = (f32[4,8,256,128]{2,1,3,0:T(8,128)S(1)}, f32[4,8,256,128]{2,1,3,0:T(8,128)}, u32[]{:S(2)}) copy-start(f32[4,8,256,128]{2,1,3,0:T(8,128)} %get-tuple-element.9) | copy-start | bytes 12582916
  107.6 4.0 %copy-start.3 = (f32[4,8,256,128]{2,1,3,0:T(8,128)S(1)}, f32[4,8,256,128]{2,1,3,0:T(8,128)}, u32[]{:S(2)}) copy-start(f32[4,8,256,128]{2,1,3,0:T(8,128)} %copy.76) | copy-start | bytes 12582916
  107.6 4.0 %copy-start.7 = (f32[4,256,128]{1,2,0:T(8,128)S(1)}, f32[4,256,128]{1,2,0:T(8,128)}, u32[]{:S(2)}) copy-start(f32[4,256,128]{1,2,0:T(8,128)} %copy.61) | copy-start | bytes 1572868
  107.6 4.1 %copy-start.8 = (f32[4,256,128]{1,2,0:T(8,128)S(1)}, f32[4,256,128]{1,2,0:T(8,128)}, u32[]{:S(2)}) copy-start(f32[4,256,128]{1,2,0:T(8,128)} %copy.59) | copy-start | bytes 1572868
where the time goes:
time: 237 us; the launch traced here: 236 us
  blocking collectives  83 us (35%)
  local copies, waits for them, and re-layouts  55.8 us (24%)
  other arithmetic  52.7 us (22%)
  starting transfers between devices  23.3 us (10%)
  matrix products  18.1 us (8%)
    psum x1, blocking collectives, local(): lower = jnp.linalg.cholesky(lax.psum(local_gram, ('gx', 'gy')))  83 us
    mul x2, other arithmetic, tendency(): grad_x = 0.5 * (east - west)  17.8 us
    ppermute x4, starting transfers between devices, with_halo(): lax.ppermute(tail, axis, [(i, (i + 1) % count) for i in range(ends)])  13.4 us
    dot_general x1, matrix products, local(): jnp.einsum('vcxy,vdxy->cd', response, response, precision=lax.Precision.H...  12.6 us
    unnamed x30, local copies, waits for them, and re-layouts  12.3 us
    mul x5, local copies, waits for them, and re-layouts, tendency(): mixing = coupling[:, 0][:, None] * center[0][None]  12.1 us
    add x1, other arithmetic, local(): middle = forcing + STEP * first  11.5 us
    add x1, other arithmetic, local(): response = forcing + 0.5 * STEP * (first + second)  11.4 us
  transfers between devices with their start and end apart: 8, of which 1 were waited for; matrix products, arithmetic and copies ran while one was open for 15% of the time, Pallas kernels for 0%

commit v1 on v0

--- a/solution.py
+++ b/solution.py
@@ -59,7 +59,7 @@
         jnp.einsum("vcxy,vdxy->cd", response, response, precision=lax.Precision.HIGHEST)
         / rows_total
     )
-    lower = jnp.linalg.cholesky(lax.psum(local_gram, ("gx", "gy")))
+    lower = jnp.linalg.cholesky(jnp.sum(lax.all_gather(local_gram, ("gx", "gy")), axis=0))
     identity = jnp.eye(lower.shape[0], dtype=lower.dtype)
     inverse = lax.linalg.triangular_solve(lower, identity, left_side=True, lower=True)
     basis = jnp.einsum("cd,vdxy->vcxy", inverse, response, precision=lax.Precision.HIGHEST)

time: 237 us -> 266 us (1.12)
  blocking collectives: 83 us -> 110 us
    all_gather x0 -> x1, blocking collectives: none -> 110 us  [local(): lax.all_gather(local_gram, ('gx', 'gy'))]
    psum x1 -> x0, blocking collectives: 83 us -> none  [local(): lower = jnp.linalg.cholesky(lax.psum(local_gram, ('gx', 'gy')))]
  transfers between devices with their start and end apart: 8 -> 8, of which waited for: 1 -> 1; matrix products, arithmetic and copies ran while one was open for 15% -> 13% of each run, Pallas kernels for 0% -> 0%
where the time goes in v1:
time: 266 us; the launch traced here: 263 us
  blocking collectives  110 us (41%)
  local copies, waits for them, and re-layouts  55.8 us (21%)
  other arithmetic  53 us (20%)
  starting transfers between devices  23.3 us (9%)
  matrix products  18.7 us (7%)
    all_gather x1, blocking collectives, local(): lax.all_gather(local_gram, ('gx', 'gy'))  110 us
    mul x2, other arithmetic, tendency(): grad_x = 0.5 * (east - west)  17.8 us
    ppermute x4, starting transfers between devices, with_halo(): lax.ppermute(tail, axis, [(i, (i + 1) % count) for i in range(ends)])  13.4 us
    dot_general x1, matrix products, local(): jnp.einsum('vcxy,vdxy->cd', response, response, precision=lax.Precision.H...  13.1 us
    unnamed x30, local copies, waits for them, and re-layouts  12.3 us
    mul x5, local copies, waits for them, and re-layouts, tendency(): mixing = coupling[:, 0][:, None] * center[0][None]  12.1 us
    add x1, other arithmetic, local(): middle = forcing + STEP * first  11.5 us
    add x1, other arithmetic, local(): response = forcing + 0.5 * STEP * (first + second)  11.4 us
  transfers between devices with their start and end apart: 8, of which 1 were waited for; matrix products, arithmetic and copies ran while one was open for 13% of the time, Pallas kernels for 0%

profile of v1, /device:TPU:1, one launch (start us, length us, event | category | flops | bytes accessed | tf_op | source)
XLA Modules:
  0.0 263.3 jit_solution(1248384867891236437)
XLA Ops:
  1.6 5.1 %collective-permute-start = (f32[4,8,1,128]{3,1,2,0:T(8,128)S(1)}, f32[4,8,1,128]{3,1,2,0:T(8,128)S(1)}, u32[]{:S(2)}, u32[]{:S(2)}) collective-permute-start(f32[4,8,1,128]{3,1,2,0:T(8,128)S(1)} %bitcast.61), channel_id=1, source_target_pairs={{16,0},{32,16},{48,32},{64,48},{80,64},{96,80},{112,96},{128,112},... | collective-permute-start | bytes 49160 | tf_op jit(solution)/shard_map/ppermute | solution.py:19
  6.8 2.1 collective-permute-start.1
  8.8 3.8 %slice_bitcast_fusion.7 = (f32[8,256,128]{2,1,0:T(8,128)}, f32[8,256,128]{2,1,0:T(8,128)S(1)}, f32[8,256,128]{2,1,0:T(8,128)}, f32[8,256,128]{2,1,0:T(8,128)}) fusion(f32[4,8,256,128]{3,2,1,0:T(8,128)} %param.5), kind=kLoop, calls=%fused_computation.52 | loop fusion | bytes 8388608 | tf_op jit(solution)/shard_map/mul | solution.py:40
  14.1 5.4 %copy.74 = f32[4,8,256,128]{2,1,3,0:T(8,128)} copy(f32[4,8,256,128]{3,2,1,0:T(8,128)} %param.5) | data formatting | bytes 8388608 | tf_op args[0]
  23.8 3.6 %collective-permute-start.3 = (f32[4,8,258,1]{2,1,3,0:T(8,128)}, f32[4,8,258,1]{2,1,3,0:T(8,128)}, u32[]{:S(2)}, u32[]{:S(2)}) collective-permute-start(f32[4,8,258,1]{2,1,3,0:T(8,128)} %get-tuple-element.16), channel_id=1, source_target_pairs={{0,1},{1,2},{2,3},{3,4},{4,5},{5,6},{6,7},{7,8},{8,9},{9,10},{10,1... | collective-permute-start | bytes 99080 | tf_op jit(solution)/shard_map/ppermute | solution.py:17
  31.4 2.6 copy.62
  35.3 2.6 copy.60
  37.9 2.0 copy.59
  39.9 2.7 %copy.58 = f32[8,256,128]{1,0,2:T(8,128)} copy(f32[8,256,128]{2,1,0:T(8,128)} %get-tuple-element.32) | data formatting | bytes 2097152 | tf_op jit(solution)/shard_map/mul | solution.py:40
  47.6 10.8 %fusion.8 = (f32[4,8,256,128]{2,1,3,0:T(8,128)S(1)}, f32[4,8,256,128]{2,1,3,0:T(8,128)S(1)}) fusion(f32[4,8,1,128]{2,1,3,0:T(8,128)S(1)} %copy.46, f32[4,8,256,128]{2,1,3,0:T(8,128)} %copy.74, f32[4,8,1,128]{2,1,3,0:T(8,128)} %copy.48, f32[4,8,258,1]{2,1,3,0:T(8,128)} %collective-permute-done.3, f32[4,8,258,1]{2,1,3,0:T(8,128)} %collective-permute-done.2), kind=kLoop, calls=%fused_computation.27 | loop fusion | flops 12582912 | bytes 12681728 | tf_op jit(solution)/shard_map/mul | solution.py:32
  62.4 11.5 %multiply_add_fusion = (f32[4,8,256,128]{2,1,3,0:T(8,128)S(1)}, f32[4,8,256,128]{2,1,3,0:T(8,128)}) fusion(f32[4,8,256,128]{2,1,3,0:T(8,128)S(1)} %copy-done.2, f32[8,256,128]{1,0,2:T(8,128)} %copy.64, f32[4,256,128]{1,2,0:T(8,128)S(1)} %copy.63, f32[8,256,128]{1,0,2:T(8,128)} %copy.62, f32[4,256,128]{1,2,0:T(8,128)S(1)} %copy.61, f32[8,256,128]{1,0,2:T(8,128)} %copy.60, ...), kind=kLoop, calls=%fused_computation.25 | loop fusion | flops 36700160 | bytes 22512128 | tf_op jit(solution)/shard_map/add | solution.py:52
  73.9 2.5 fusion.18
  76.6 2.2 copy.67
  82.0 3.6 %collective-permute-start.5 = (f32[4,8,1,128]{3,1,2,0:T(8,128)}, f32[4,8,1,128]{3,1,2,0:T(8,128)}, u32[]{:S(2)}, u32[]{:S(2)}) collective-permute-start(f32[4,8,1,128]{3,1,2,0:T(8,128)} %copy.69), channel_id=1, source_target_pairs={{0,16},{16,32},{32,48},{48,64},{64,80},{80,96},{96,112},{112,128},... | collective-permute-start | bytes 49160 | tf_op jit(solution)/shard_map/ppermute | solution.py:17
  87.1 2.8 %copy.70 = f32[4,8,1,128]{2,1,3,0:T(8,128)} copy(f32[4,8,1,128]{3,1,2,0:T(8,128)} %collective-permute-done.5) | data formatting | bytes 32768 | tf_op jit(solution)/shard_map/ppermute | solution.py:17
  90.9 4.1 %collective-permute-start.7 = (f32[4,8,258,1]{2,1,3,0:T(8,128)S(1)}, f32[4,8,258,1]{2,1,3,0:T(8,128)S(1)}, u32[]{:S(2)}, u32[]{:S(2)}) collective-permute-start(f32[4,8,258,1]{2,1,3,0:T(8,128)S(1)} %get-tuple-element.12), channel_id=1, source_target_pairs={{0,1},{1,2},{2,3},{3,4},{4,5},{5,6},{6,7},{7,8},{8,9},{9,10},{10,1... | collective-permute-start | bytes 99080 | tf_op jit(solution)/shard_map/ppermute | solution.py:17
  100.7 6.9 %fusion.10 = (f32[4,8,256,128]{2,1,3,0:T(8,128)}, f32[4,8,256,128]{2,1,3,0:T(8,128)}) fusion(f32[4,8,1,128]{2,1,3,0:T(8,128)S(1)} %copy.68, f32[4,8,256,128]{2,1,3,0:T(8,128)S(1)} %copy-done.1, f32[4,8,1,128]{2,1,3,0:T(8,128)S(1)} %copy-done.5, f32[4,8,258,1]{2,1,3,0:T(8,128)S(1)} %collective-permute-done.7, f32[4,8,258,1]{2,1,3,0:T(8,128)S(1)} %collective-permute-done.6), kind=kLoop, calls=%fused_computation.29 | loop fusion | flops 12582912 | bytes 12681728 | tf_op jit(solution)/shard_map/mul | solution.py:32
  107.6 4.0 %slice_multiply_fusion.1 = (f32[1,8,256,128]{2,1,3,0:T(8,128)S(1)}, f32[1,8,256,128]{2,1,3,0:T(8,128)}, f32[1,8,256,128]{2,1,3,0:T(8,128)}) fusion(f32[4,8,256,128]{2,1,3,0:T(8,128)} %get-tuple-element.10, f32[256,128]{0,1:T(8,128)S(1)} %copy-done.11, f32[4,8,256,128]{2,1,3,0:T(8,128)} %get-tuple-element.11), kind=kLoop, calls=%fused_computation.41 | loop fusion | flops 1048576 | bytes 7471104 | tf_op jit(solution)/shard_map/mul | solution.py:38
  111.8 11.4 %fusion.6 = f32[4,8,256,128]{2,1,3,0:T(8,128)} fusion(f32[4,8,256,128]{2,1,3,0:T(8,128)S(1)} %copy-done.3, f32[4,8,256,128]{2,1,3,0:T(8,128)S(1)} %copy-done.6, f32[1,8,256,128]{2,1,3,0:T(8,128)} %get-tuple-element.19, f32[1,8,256,128]{2,1,3,0:T(8,128)} %get-tuple-element.20, f32[1,8,256,128]{2,1,3,0:T(8,128)S(1)} %get-tuple-element.18, ...), kind=kLoop, calls=%fused_computation.24 | loop fusion | flops 37748736 | bytes 26706432 | tf_op jit(solution)/shard_map/add | solution.py:54
  123.2 5.5 %copy.77 = f32[4,8,256,128]{3,1,2,0:T(8,128)} copy(f32[4,8,256,128]{2,1,3,0:T(8,128)} %fusion.6) | data formatting | bytes 8388608 | tf_op jit(solution)/shard_map/add | solution.py:54
  128.7 13.1 %fusion.11 = f32[8,8]{1,0:T(8,128)S(1)} fusion(f32[4,8,256,128]{2,1,3,0:T(8,128)} %fusion.6), kind=kOutput, calls=%fused_computation.35 | convolution fusion | flops 100663360 | bytes 4194560 | tf_op jit(solution)/shard_map/vcxy,vdxy->cd/dot_general | solution.py:59
  141.8 109.6 %all-gather = f32[2048,8]{1,0:T(8,128)S(1)} all-gather(f32[8,8]{1,0:T(8,128)S(1)} %fusion.11), channel_id=2, replica_groups=mesh['gx'=16,'gy'=16] {'gx','gy'}, dimensions={0}, use_global_device_ids=true | all-gather | bytes 65792 | tf_op jit(solution)/shard_map/all_gather | solution.py:62
  254.6 5.3 %convolution_bitcast_fusion = f32[4,8,256,128]{3,1,2,0:T(8,128)S(1)} fusion(f32[4,8,256,128]{3,1,2,0:T(8,128)} %copy.77, f32[8,8,1,1]{1,0,3,2:T(8,128)S(1)} %convolution_bitcast_fusion.1), kind=kOutput, calls=%fused_computation.30 | convolution fusion | flops 100663296 | bytes 8388864 | tf_op jit(solution)/shard_map/cd,vdxy->vcxy/dot_general | solution.py:65
  259.9 2.8 %copy.78 = f32[4,8,256,128]{3,2,1,0:T(8,128)} copy(f32[4,8,256,128]{3,1,2,0:T(8,128)S(1)} %convolution_bitcast_fusion) | data formatting | bytes 8388608
  (67 shorter events, 36.3 us)
Async XLA Ops:
  1.6 17.9 %collective-permute-start = (f32[4,8,1,128]{3,1,2,0:T(8,128)S(1)}, f32[4,8,1,128]{3,1,2,0:T(8,128)S(1)}, u32[]{:S(2)}, u32[]{:S(2)}) collective-permute-start(f32[4,8,1,128]{3,1,2,0:T(8,128)S(1)} %bitcast.61), channel_id=1, source_target_pairs={{16,0},{32,16},{48,32},{64,48},{80,64},{96,80},{112,96},{128,112},... | collective-permute-start | bytes 49160 | tf_op jit(solution)/shard_map/ppermute | solution.py:19
  6.7 5.9 %copy-start.9 = (f32[4,4,256,128]{3,2,1,0:T(8,128)S(1)}, f32[4,4,256,128]{3,2,1,0:T(8,128)}, u32[]{:S(2)}) copy-start(f32[4,4,256,128]{3,2,1,0:T(8,128)} %param.9) | copy-start | bytes 6291460
  6.8 13.5 %collective-permute-start.1 = (f32[4,8,1,128]{3,1,2,0:T(8,128)S(1)}, f32[4,8,1,128]{3,1,2,0:T(8,128)S(1)}, u32[]{:S(2)}, u32[]{:S(2)}) collective-permute-start(f32[4,8,1,128]{3,1,2,0:T(8,128)S(1)} %bitcast.60), channel_id=1, source_target_pairs={{0,16},{16,32},{32,48},{48,64},{64,80},{80,96},{96,112},{112,128},... | collective-permute-start | bytes 49160 | tf_op jit(solution)/shard_map/ppermute | solution.py:17
  22.3 6.5 %copy-start.12 = (f32[2,256,128]{2,1,0:T(8,128)S(1)}, f32[2,256,128]{2,1,0:T(8,128)}, u32[]{:S(2)}) copy-start(f32[2,256,128]{2,1,0:T(8,128)} %param.6) | copy-start | bytes 786436
  23.8 23.7 %collective-permute-start.3 = (f32[4,8,258,1]{2,1,3,0:T(8,128)}, f32[4,8,258,1]{2,1,3,0:T(8,128)}, u32[]{:S(2)}, u32[]{:S(2)}) collective-permute-start(f32[4,8,258,1]{2,1,3,0:T(8,128)} %get-tuple-element.16), channel_id=1, source_target_pairs={{0,1},{1,2},{2,3},{3,4},{4,5},{5,6},{6,7},{7,8},{8,9},{9,10},{10,1... | collective-permute-start | bytes 99080 | tf_op jit(solution)/shard_map/ppermute | solution.py:17
  27.4 20.1 %collective-permute-start.2 = (f32[4,8,258,1]{2,1,3,0:T(8,128)}, f32[4,8,258,1]{2,1,3,0:T(8,128)}, u32[]{:S(2)}, u32[]{:S(2)}) collective-permute-start(f32[4,8,258,1]{2,1,3,0:T(8,128)} %get-tuple-element.17), channel_id=1, source_target_pairs={{1,0},{2,1},{3,2},{4,3},{5,4},{6,5},{7,6},{8,7},{9,8},{10,9},{11,1... | collective-permute-start | bytes 99080 | tf_op jit(solution)/shard_map/ppermute | solution.py:19
  47.5 10.9 %copy-start.10 = (f32[256,128]{0,1:T(8,128)S(1)}, f32[256,128]{0,1:T(8,128)}, u32[]{:S(2)}) copy-start(f32[256,128]{0,1:T(8,128)} %copy.56) | copy-start | bytes 393220
  58.4 3.3 %copy-start.2 = (f32[4,8,256,128]{2,1,3,0:T(8,128)S(1)}, f32[4,8,256,128]{2,1,3,0:T(8,128)}, u32[]{:S(2)}) copy-start(f32[4,8,256,128]{2,1,3,0:T(8,128)} %copy.74) | copy-start | bytes 12582916
  58.4 4.0 %copy-start.4 = (f32[4,8,1,128]{2,1,3,0:T(8,128)S(1)}, f32[4,8,1,128]{2,1,3,0:T(8,128)}, u32[]{:S(2)}) copy-start(f32[4,8,1,128]{2,1,3,0:T(8,128)} %copy.48) | copy-start | bytes 49156
  73.9 2.7 %copy-start = (f32[4,8,256,128]{2,1,3,0:T(8,128)}, f32[4,8,256,128]{2,1,3,0:T(8,128)S(1)}, u32[]{:S(2)}) copy-start(f32[4,8,256,128]{2,1,3,0:T(8,128)S(1)} %get-tuple-element.8) | copy-start | bytes 12582916
  78.8 6.8 %collective-permute-start.4 = (f32[4,8,1,128]{3,1,2,0:T(8,128)S(1)}, f32[4,8,1,128]{3,1,2,0:T(8,128)}, u32[]{:S(2)}, u32[]{:S(2)}) collective-permute-start(f32[4,8,1,128]{3,1,2,0:T(8,128)S(1)} %copy.67), channel_id=1, source_target_pairs={{16,0},{32,16},{48,32},{64,48},{80,64},{96,80},{112,96},{128,112},... | collective-permute-start | bytes 49160 | tf_op jit(solution)/shard_map/ppermute | solution.py:19
  82.0 5.1 %collective-permute-start.5 = (f32[4,8,1,128]{3,1,2,0:T(8,128)}, f32[4,8,1,128]{3,1,2,0:T(8,128)}, u32[]{:S(2)}, u32[]{:S(2)}) collective-permute-start(f32[4,8,1,128]{3,1,2,0:T(8,128)} %copy.69), channel_id=1, source_target_pairs={{0,16},{16,32},{32,48},{48,64},{64,80},{80,96},{96,112},{112,128},... | collective-permute-start | bytes 49160 | tf_op jit(solution)/shard_map/ppermute | solution.py:17
  89.8 6.8 %copy-start.1 = (f32[4,8,256,128]{2,1,3,0:T(8,128)S(1)}, f32[4,8,256,128]{2,1,3,0:T(8,128)}, u32[]{:S(2)}) copy-start(f32[4,8,256,128]{2,1,3,0:T(8,128)} %copy-done) | copy-start | bytes 12582916
  90.9 7.8 %collective-permute-start.7 = (f32[4,8,258,1]{2,1,3,0:T(8,128)S(1)}, f32[4,8,258,1]{2,1,3,0:T(8,128)S(1)}, u32[]{:S(2)}, u32[]{:S(2)}) collective-permute-start(f32[4,8,258,1]{2,1,3,0:T(8,128)S(1)} %get-tuple-element.12), channel_id=1, source_target_pairs={{0,1},{1,2},{2,3},{3,4},{4,5},{5,6},{6,7},{7,8},{8,9},{9,10},{10,1... | collective-permute-start | bytes 99080 | tf_op jit(solution)/shard_map/ppermute | solution.py:17
  95.0 5.7 %copy-start.5 = (f32[4,8,1,128]{2,1,3,0:T(8,128)S(1)}, f32[4,8,1,128]{2,1,3,0:T(8,128)}, u32[]{:S(2)}) copy-start(f32[4,8,1,128]{2,1,3,0:T(8,128)} %copy.70) | copy-start | bytes 49156
  95.0 5.7 %collective-permute-start.6 = (f32[4,8,258,1]{2,1,3,0:T(8,128)S(1)}, f32[4,8,258,1]{2,1,3,0:T(8,128)S(1)}, u32[]{:S(2)}, u32[]{:S(2)}) collective-permute-start(f32[4,8,258,1]{2,1,3,0:T(8,128)S(1)} %get-tuple-element.13), channel_id=1, source_target_pairs={{1,0},{2,1},{3,2},{4,3},{5,4},{6,5},{7,6},{8,7},{9,8},{10,9},{11,1... | collective-permute-start | bytes 99080 | tf_op jit(solution)/shard_map/ppermute | solution.py:19
  98.6 9.0 %copy-start.11 = (f32[256,128]{0,1:T(8,128)S(1)}, f32[256,128]{0,1:T(8,128)}, u32[]{:S(2)}) copy-start(f32[256,128]{0,1:T(8,128)} %copy.56) | copy-start | bytes 393220
  100.7 10.9 %copy-start.6 = (f32[4,8,256,128]{2,1,3,0:T(8,128)S(1)}, f32[4,8,256,128]{2,1,3,0:T(8,128)}, u32[]{:S(2)}) copy-start(f32[4,8,256,128]{2,1,3,0:T(8,128)} %get-tuple-element.9) | copy-start | bytes 12582916
  107.6 4.0 %copy-start.3 = (f32[4,8,256,128]{2,1,3,0:T(8,128)S(1)}, f32[4,8,256,128]{2,1,3,0:T(8,128)}, u32[]{:S(2)}) copy-start(f32[4,8,256,128]{2,1,3,0:T(8,128)} %copy.74) | copy-start | bytes 12582916
  107.6 4.0 %copy-start.7 = (f32[4,256,128]{1,2,0:T(8,128)S(1)}, f32[4,256,128]{1,2,0:T(8,128)}, u32[]{:S(2)}) copy-start(f32[4,256,128]{1,2,0:T(8,128)} %copy.59) | copy-start | bytes 1572868
  107.6 4.1 %copy-start.8 = (f32[4,256,128]{1,2,0:T(8,128)S(1)}, f32[4,256,128]{1,2,0:T(8,128)}, u32[]{:S(2)}) copy-start(f32[4,256,128]{1,2,0:T(8,128)} %copy.57) | copy-start | bytes 1572868
